TPU v7x, 32 devices: a whole 2x2x4 slice. The times are simulated.
32 devices in a mesh: groups: 2 (over y), seq: 4 (over z), tensor: 4 (over x, core).
Axes of the slice: x: 2, y: 2, z: 4, core: 2. Of those that a mesh axis runs over, the one named last changes fastest.
Arguments:
- x_in: bfloat16 [4096, 5120], P(('groups', 'seq'), 'tensor'), parts along dimension 0, may hold values from -6 to 6
- z_gate: bfloat16 [4096, 5120], P(('groups', 'seq'), 'tensor'), parts along dimension 0, may hold values from -32 to 32
- bc_in: bfloat16 [4096, 256], P(('groups', 'seq')), parts along dimension 0, may hold values from -6 to 6
- step_size: float32 [80, 4096], P('tensor', ('groups', 'seq')), parts along dimension 1, may hold values from 0 to 0.4
- log_keep: float32 [80, 4096], P('tensor', ('groups', 'seq')), parts along dimension 1, may hold values from -1 to 0
- skip_gain: float32 [80], P('tensor'), may hold values from 0.5 to 2
- conv_x: bfloat16 [4, 5120], P(None, 'tensor'), may hold values from -3 to 3
- conv_bc: bfloat16 [4, 256], replicated, may hold values from -3 to 3
- norm_gain: float32 [5120], P('tensor'), may hold values from 0.1 to 1.9
- seg_ends: int32 [1024], P(('groups', 'seq')), parts along dimension 0, may hold values from 0 to 2047, as said below
- pool_query: bfloat16 [320, 5120], P(('groups', 'seq'), 'tensor'), parts along dimension 0, may hold values from -64 to 64
- pool_start: int32 [320], P(('groups', 'seq')), parts along dimension 0, may hold values from 0 to 255, as said below
- pool_stop: int32 [320], P(('groups', 'seq')), parts along dimension 0, may hold values from 64 to 512
Outputs:
- mixed_seq: bfloat16 [4096, 5120], P(('groups', 'seq'), 'tensor'), parts along dimension 0
- pooled: float32 [320, 5120], P(('groups', 'seq'), 'tensor'), parts along dimension 0
There are 2 independent parts, one for each index of `groups`. A program takes and returns all parts, laid end to end along the dimension named above; an argument that names none is the same for every part. Nothing has to cross between parts.
Inputs may be any that keep to these rules, and one draw needn't show every extreme that they name: The tokens fall into blocks of 512; block b holds exactly the 128 segment ends seg_ends[b * 128] to seg_ends[(b + 1) * 128 - 1], strictly increasing. pool_start < pool_stop for every pooled row.
All inputs are finite; a program needn't handle non-finite values.
Results may differ from a plain program's by a relative error of at most 0.039.
Values may be sent and summed in bfloat16 or wider, within the bound.
No kernel may reach another device: no remote copies, remote signals or barrier semaphores. Data moves between devices by JAX's collectives and lax.ppermute only.
A program may use at most 64 MiB of HBM per device.

v0:
```python
import math
import jax
import jax.numpy as jnp
from jax import lax
from jax.sharding import PartitionSpec as P

STRETCH = 256
POOL_HEADS = 32
EPSILON = 1e-05
MASKED = -1e30


def passed_along(value, axis, steps):
    count = lax.axis_size(axis)
    leading, last = (max(0, -steps), min(count, count - steps))
    return lax.ppermute(value, axis, [(source, source + steps) for source in range(leading, last)])


def silu_act(values):
    return values / (1.0 + jnp.exp(-values))


def causal_conv(before, current, weights):
    kernel_width = weights.shape[0]
    length = current.shape[0]
    padded = jnp.concatenate([before, current], axis=0)
    summed = jnp.zeros(current.shape, jnp.float32)
    for offset in range(kernel_width):
        summed = summed + padded[offset : offset + length].astype(jnp.float32) * weights[
            offset
        ].astype(jnp.float32)
    return silu_act(summed).astype(jnp.bfloat16)


def stretch_local(x_block, b_block, c_block, step_block, keep_block):
    block_len = x_block.shape[0]
    cumul_keep = jnp.cumsum(keep_block, axis=1)
    lower_mask = lax.broadcasted_iota(jnp.int32, (block_len, block_len), 0) >= lax.broadcasted_iota(
        jnp.int32, (block_len, block_len), 1
    )
    inner_prod = jnp.einsum("is,js->ij", c_block, b_block, preferred_element_type=jnp.float32)
    spread = cumul_keep[:, :, None] - cumul_keep[:, None, :]
    decay_mask = jnp.where(lower_mask[None], jnp.exp(jnp.where(lower_mask[None], spread, 0.0)), 0.0)
    mixing = (decay_mask * inner_prod[None] * step_block[:, None, :]).astype(jnp.bfloat16)
    intra_part = jnp.einsum("hij,jhp->ihp", mixing, x_block, preferred_element_type=jnp.float32)
    tail_weight = jnp.exp(cumul_keep[:, -1:] - cumul_keep) * step_block
    weighted = (tail_weight.T[:, :, None] * x_block.astype(jnp.float32)).astype(jnp.bfloat16)
    stretch_state = jnp.einsum("jhp,js->hps", weighted, b_block, preferred_element_type=jnp.float32)
    return (intra_part, stretch_state, cumul_keep)


def combine(earlier, later):
    return (earlier[0] * jnp.exp(later[1])[:, None, None] + later[0], earlier[1] + later[1])


def exclusive_scan(state, decay, axis):
    count = lax.axis_size(axis)
    window = (state, decay)
    before = (jnp.zeros_like(state), jnp.zeros_like(decay))
    shift = 1
    while shift < count:
        sent_state = passed_along(window[0].astype(jnp.bfloat16), axis, shift)
        sent_decay = passed_along(window[1], axis, shift)
        received = (sent_state.astype(jnp.float32), sent_decay)
        before = combine(received, before)
        if shift * 2 < count:
            window = combine(received, window)
        shift *= 2
    return before[0]


def read_state(c_block, state_in):
    state_high = state_in.astype(jnp.bfloat16)
    state_low = (state_in - state_high.astype(jnp.float32)).astype(jnp.bfloat16)
    high_part = jnp.einsum("is,hps->ihp", c_block, state_high, preferred_element_type=jnp.float32)
    low_part = jnp.einsum("is,hps->ihp", c_block, state_low, preferred_element_type=jnp.float32)
    return high_part + low_part


def local(
    x_in,
    z_gate,
    bc_in,
    step_size,
    log_keep,
    skip_gain,
    conv_x,
    conv_bc,
    norm_gain,
    seg_ends,
    pool_query,
    pool_start,
    pool_stop,
):
    tok_rows = x_in.shape[0]
    channels = x_in.shape[1]
    heads_local = step_size.shape[0]
    head_width = channels // heads_local
    state_width = bc_in.shape[1] // 2
    rim_rows = conv_x.shape[0] - 1
    seq_count = lax.axis_size("seq")
    queries_all = lax.all_gather(pool_query, "seq", axis=0, tiled=True)
    start_all = lax.all_gather(pool_start, "seq", axis=0, tiled=True)
    stop_all = lax.all_gather(pool_stop, "seq", axis=0, tiled=True)
    edge_rows = jnp.concatenate([x_in[tok_rows - rim_rows :], bc_in[tok_rows - rim_rows :]], axis=1)
    before = passed_along(edge_rows, "seq", 1)
    x_conv = causal_conv(before[:, :channels], x_in, conv_x)
    bc_conv = causal_conv(before[:, channels:], bc_in, conv_bc)
    b_mat = bc_conv[:, :state_width]
    c_mat = bc_conv[:, state_width:]
    x_heads = x_conv.reshape(tok_rows, heads_local, head_width)
    stretch_count = tok_rows // STRETCH
    entry_state = jnp.zeros((heads_local, head_width, state_width), jnp.float32)
    decay_total = jnp.zeros((heads_local,), jnp.float32)
    saved_parts = []
    for block_index in range(stretch_count):
        first_row = block_index * STRETCH
        last_row = first_row + STRETCH
        intra_part, stretch_state, cumul_keep = stretch_local(
            x_heads[first_row:last_row],
            b_mat[first_row:last_row],
            c_mat[first_row:last_row],
            step_size[:, first_row:last_row],
            log_keep[:, first_row:last_row],
        )
        saved_parts.append((intra_part, cumul_keep, entry_state, decay_total))
        entry_state = jnp.exp(cumul_keep[:, -1])[:, None, None] * entry_state + stretch_state
        decay_total = decay_total + cumul_keep[:, -1]
    incoming = exclusive_scan(entry_state, decay_total, "seq")
    pieces_out = []
    for block_index in range(stretch_count):
        intra_part, cumul_keep, entry_part, decay_part = saved_parts[block_index]
        first_row = block_index * STRETCH
        state_in = entry_part + jnp.exp(decay_part)[:, None, None] * incoming
        from_state = read_state(c_mat[first_row : first_row + STRETCH], state_in)
        pieces_out.append(intra_part + jnp.exp(cumul_keep).T[:, :, None] * from_state)
    ssd_out = jnp.concatenate(pieces_out, axis=0) + skip_gain[None, :, None] * x_heads.astype(
        jnp.float32
    )
    gated = ssd_out.reshape(tok_rows, channels) * silu_act(z_gate.astype(jnp.float32))
    square_sum = lax.psum(jnp.sum(gated * gated, axis=1), "tensor")
    width_all = channels * lax.axis_size("tensor")
    mixed_seq = (
        gated * lax.rsqrt(square_sum / width_all + EPSILON)[:, None] * norm_gain[None, :]
    ).astype(jnp.bfloat16)
    local_ends = seg_ends - lax.axis_index("seq") * tok_rows
    summaries = jnp.take(mixed_seq, local_ends, axis=0)
    pool_heads_local = POOL_HEADS // lax.axis_size("tensor")
    pool_width = channels // pool_heads_local
    scale_factor = 1.0 / math.sqrt(pool_width)
    pools_local = pool_query.shape[0]
    pools_all = queries_all.shape[0]
    segs_local = summaries.shape[0]
    queries = queries_all.reshape(pools_all, pool_heads_local, pool_width)
    seg_index = lax.axis_index("seq") * segs_local + lax.iota(jnp.int32, segs_local)
    inside = (seg_index[None, :] >= start_all[:, None]) & (seg_index[None, :] < stop_all[:, None])
    keys_block = summaries.reshape(segs_local, pool_heads_local, pool_width)
    logits = (
        jnp.einsum("pad,rad->apr", queries, keys_block, preferred_element_type=jnp.float32)
        * scale_factor
    )
    logits = jnp.where(inside[None], logits, MASKED)
    peak = jnp.max(logits, axis=2)
    expo = jnp.where(inside[None], jnp.exp(logits - peak[:, :, None]), 0.0)
    denom = jnp.sum(expo, axis=2)
    numer = jnp.einsum(
        "apr,rad->pad", expo.astype(jnp.bfloat16), keys_block, preferred_element_type=jnp.float32
    )
    numer_sent = lax.all_to_all(
        numer.reshape(pools_all, channels).astype(jnp.bfloat16), "seq", 0, 0, tiled=True
    )
    stats = jnp.concatenate([peak.T, denom.T], axis=1)
    stats_sent = lax.all_to_all(stats, "seq", 0, 0, tiled=True)
    numer_parts = numer_sent.astype(jnp.float32).reshape(
        seq_count, pools_local, pool_heads_local, pool_width
    )
    stats_parts = stats_sent.reshape(seq_count, pools_local, 2, pool_heads_local)
    peak_parts = stats_parts[:, :, 0]
    denom_parts = stats_parts[:, :, 1]
    peak_all = jnp.max(peak_parts, axis=0)
    rescale = jnp.exp(peak_parts - peak_all[None])
    denom_all = jnp.sum(rescale * denom_parts, axis=0)
    numer_all = jnp.sum(rescale[:, :, :, None] * numer_parts, axis=0)
    pooled = (numer_all / denom_all[:, :, None]).reshape(pools_local, channels)
    return (mixed_seq, pooled)


def solution(mesh):
    in_specs = (
        P(("groups", "seq"), "tensor"),
        P(("groups", "seq"), "tensor"),
        P(("groups", "seq"), None),
        P("tensor", ("groups", "seq")),
        P("tensor", ("groups", "seq")),
        P("tensor"),
        P(None, "tensor"),
        P(),
        P("tensor"),
        P(("groups", "seq")),
        P(("groups", "seq"), "tensor"),
        P(("groups", "seq")),
        P(("groups", "seq")),
    )
    out_specs = (P(("groups", "seq"), "tensor"), P(("groups", "seq"), "tensor"))
    return jax.shard_map(local, mesh=mesh, in_specs=in_specs, out_specs=out_specs, check_vma=False)
```

profile of v0, /device:TPU:0, one launch (start us, length us, event | category | flops | bytes accessed | tf_op | source)
XLA Modules:
  0.0 130.5 jit_solution(8809013497023641823)
XLA Ops:
  0.6 0.8 slice.127
  1.4 0.7 slice.126
  2.2 5.0 %collective-permute-start = (bf16[3,1536]{1,0:T(4,128)(2,1)S(1)}, bf16[3,1536]{1,0:T(4,128)(2,1)S(1)}, u32[]{:S(2)}, u32[]{:S(2)}) collective-permute-start(bf16[3,1536]{1,0:T(4,128)(2,1)S(1)} %pad_maximum_fusion.3), channel_id=1, source_target_pairs={{0,4},{4,8},{8,12},{1,5},{5,9},{9,13},{2,6},{6,10},{10,14},{3,7},{... | collective-permute-start | bytes 27656 | tf_op jit(solution)/shard_map/ppermute | solution.py:16
  7.2 0.8 fusion.82
  7.9 0.6 reduce-window.14
  10.6 3.5 %collective-permute-start.3 = (f32[20]{0:T(128)S(1)}, f32[20]{0:T(128)S(1)}, u32[]{:S(2)}, u32[]{:S(2)}) collective-permute-start(f32[20]{0:T(128)S(1)} %get-tuple-element.33), channel_id=1, source_target_pairs={{0,4},{4,8},{8,12},{1,5},{5,9},{9,13},{2,6},{6,10},{10,14},{3,7},{... | collective-permute-start | bytes 248 | tf_op jit(solution)/shard_map/ppermute | solution.py:16
  14.1 0.7 iota_compare_fusion
  14.8 0.9 convert_reduce_fusion.3
  15.7 1.5 %fusion.81 = (f32[20,256]{1,0:T(8,128)}, f32[256,20]{0,1:T(8,128)}, f32[256,20]{0,1:T(8,128)}, f32[20,256]{1,0:T(8,128)}, f32[256,20]{0,1:T(8,128)}, /*index=5*/f32[256,20]{0,1:T(8,128)}) fusion(f32[20,512]{1,0:T(8,128)} %param.16, f32[20,256]{1,0:T(8,128)S(1)} %bitcast.92, f32[20]{0:T(128)S(1)} %get-tuple-element.39, f32[20,256]{1,0:T(8,128)S(1)} %bitcast.95, ...), kind=kLoop, calls=%fused_computation.140 | loop fusion | flops 20480 | bytes 204960 | tf_op jit(solution)/shard_map/slice | solution.py:123
  17.2 1.4 %slice_convert_fusion.3 = (f32[1,256]{1,0:T(1,128)}, f32[1,256]{1,0:T(1,128)}, f32[1,256]{1,0:T(1,128)}, f32[1,256]{1,0:T(1,128)}) fusion(bf16[4,256]{1,0:T(4,128)(2,1)} %param.20), kind=kLoop, calls=%fused_computation.130 | loop fusion | flops 1024 | bytes 6144 | tf_op jit(solution)/shard_map/mul | solution.py:29
  18.6 15.2 %all_gather.11 = bf16[160,1280]{1,0:T(8,128)(2,1)S(1)} all-gather(bf16[40,1280]{1,0:T(8,128)(2,1)} %param.23), channel_id=1, replica_groups=mesh['groups'=2,'seq'=4,'tensor'=4] {'seq'}, dimensions={0}, use_global_device_ids=true | all-gather | bytes 512000 | tf_op jit(solution)/shard_map/all_gather | solution.py:102
  33.8 1.2 compare_and_fusion.1
  35.0 1.2 dynamic-slice
  36.8 0.9 dynamic-update-slice.1
  37.6 0.8 dynamic-update-slice
  38.5 6.6 %all-reduce.2 = (s32[160]{0:T(256)S(1)}, s32[160]{0:T(256)S(1)}) all-reduce(s32[160]{0:T(256)S(1)} %dynamic-update-slice.1, s32[160]{0:T(256)S(1)} %dynamic-update-slice), channel_id=1, replica_groups=mesh['groups'=2,'seq'=4,'tensor'=4] {'seq'}, use_global_device_ids=true, to_apply=%add.1 | all-reduce | flops 320 | bytes 2560
  45.0 0.7 compare_and_fusion
  45.7 0.7 mul.339
  46.5 1.7 %reshape.222 = bf16[160,8,160]{2,1,0:T(8,128)(2,1)} reshape(bf16[160,1280]{1,0:T(8,128)(2,1)S(1)} %all_gather.11) | data formatting | bytes 819200 | tf_op jit(solution)/shard_map/reshape | solution.py:154
  48.2 1.8 %divide_convert_fusion = bf16[512,1280]{1,0:T(8,128)(2,1)S(1)} fusion(bf16[512,1280]{1,0:T(8,128)(2,1)S(1)} %copy-done.1, bf16[3,1280]{1,0:T(4,128)(2,1)S(1)} %slice.166, f32[1280]{0:T(1024)S(1)} %get-tuple-element.4, f32[1280]{0:T(1024)S(1)} %get-tuple-element.5, f32[1280]{0:T(1024)S(1)} %get-tuple-element.3, f32[1280]{0:T(1024)S(1)} %get-tuple-element.2), kind=kLoop, calls=%fused_computation.23 | loop fusion | flops 15728640 | bytes 2649600 | tf_op jit(solution)/shard_map/convert_element_type | solution.py:32
  50.4 1.9 %divide_convert_fusion.1 = bf16[512,256]{1,0:T(8,128)(2,1)S(1)} fusion(bf16[512,256]{1,0:T(8,128)(2,1)} %param.15, bf16[3,256]{1,0:T(4,128)(2,1)S(1)} %slice.173, f32[256]{0:T(256)} %bitcast.104, f32[256]{0:T(256)} %bitcast.105, f32[256]{0:T(256)} %bitcast.103, f32[256]{0:T(256)} %bitcast.102), kind=kLoop, calls=%fused_computation.62 | loop fusion | flops 3145728 | bytes 529920 | tf_op jit(solution)/shard_map/convert_element_type | solution.py:32
  52.3 0.9 fusion.57
  53.5 1.1 convolution_add_fusion.3
  54.6 1.1 fusion.84
  55.7 3.3 %collective-permute-start.1 = (bf16[20,64,128]{2,1,0:T(8,128)(2,1)S(1)}, bf16[20,64,128]{2,1,0:T(8,128)(2,1)S(1)}, u32[]{:S(2)}, u32[]{:S(2)}) collective-permute-start(bf16[20,64,128]{2,1,0:T(8,128)(2,1)S(1)} %get-tuple-element.35), channel_id=1, source_target_pairs={{0,4},{4,8},{8,12},{1,5},{5,9},{9,13},{2,6},{6,10},{10,14},{3,7},{... | collective-permute-start | bytes 983048 | tf_op jit(solution)/shard_map/ppermute | solution.py:16
  59.1 1.7 %fusion.17 = f32[256,20,64]{0,2,1:T(8,128)S(1)} fusion(bf16[256,20,64]{0,2,1:T(8,128)(2,1)S(1)} %bitcast.88, f32[20,256]{1,0:T(8,128)S(1)} %copy-done.13, f32[256,256]{1,0:T(8,128)S(1)} %copy-done.4, f32[20,256]{1,0:T(8,128)S(1)} %bitcast.96, pred[256,256]{1,0:T(8,128)(4,1)S(1)} %copy-done.11), kind=kOutput, calls=%fused_computation.28 | convolution fusion | flops 175636480 | bytes 2334720 | tf_op jit(solution)/shard_map/hij,jhp->ihp/dot_general | solution.py:45
  60.9 3.9 %collective-permute-done.1 = bf16[20,64,128]{2,1,0:T(8,128)(2,1)S(1)} collective-permute-done((bf16[20,64,128]{2,1,0:T(8,128)(2,1)S(1)}, bf16[20,64,128]{2,1,0:T(8,128)(2,1)S(1)}, u32[]{:S(2)}, u32[]{:S(2)}) %collective-permute-start.1) | collective-permute-done | bytes 327712 | tf_op jit(solution)/shard_map/ppermute | solution.py:16
  65.0 10.0 %collective-permute-start.2 = (bf16[20,64,128]{2,1,0:T(8,128)(2,1)S(1)}, bf16[20,64,128]{2,1,0:T(8,128)(2,1)S(1)}, u32[]{:S(2)}, u32[]{:S(2)}) collective-permute-start(bf16[20,64,128]{2,1,0:T(8,128)(2,1)S(1)} %fusion.29), channel_id=1, source_target_pairs={{0,8},{4,12},{1,9},{5,13},{2,10},{6,14},{3,11},{7,15},{16,24},{20,... | collective-permute-start | bytes 983048 | tf_op jit(solution)/shard_map/ppermute | solution.py:16
  75.0 2.9 %fusion.18 = f32[256,20,64]{0,2,1:T(8,128)} fusion(bf16[256,20,64]{0,2,1:T(8,128)(2,1)S(1)} %bitcast.86, f32[20,256]{1,0:T(8,128)S(1)} %copy-done.12, f32[256,256]{1,0:T(8,128)S(1)} %fusion.61, f32[20,256]{1,0:T(8,128)S(1)} %bitcast.93, pred[256,256]{1,0:T(8,128)(4,1)S(1)} %copy-done.11), kind=kOutput, calls=%fused_computation.29 | convolution fusion | flops 175636480 | bytes 2334720 | tf_op jit(solution)/shard_map/hij,jhp->ihp/dot_general | solution.py:45
  77.9 1.6 %collective-permute-done.2 = bf16[20,64,128]{2,1,0:T(8,128)(2,1)S(1)} collective-permute-done((bf16[20,64,128]{2,1,0:T(8,128)(2,1)S(1)}, bf16[20,64,128]{2,1,0:T(8,128)(2,1)S(1)}, u32[]{:S(2)}, u32[]{:S(2)}) %collective-permute-start.2) | collective-permute-done | bytes 327712 | tf_op jit(solution)/shard_map/ppermute | solution.py:16
  79.9 1.5 %fusion.22 = f32[256,20,64]{0,2,1:T(8,128)} fusion(f32[256,20,64]{0,2,1:T(8,128)S(1)} %fusion.17, f32[256,20,64]{0,2,1:T(8,128)S(1)} %fusion.49, f32[256,20]{0,1:T(8,128)S(1)} %copy-done.10, bf16[512,256]{1,0:T(8,128)(2,1)S(1)} %divide_convert_fusion.1, f32[20,64,128]{2,1,0:T(8,128)S(1)} %convolution_add_fusion.3, ...), kind=kOutput, calls=%fused_computation.35 | convolution fusion | flops 86507520 | bytes 5334016 | tf_op jit(solution)/shard_map/is,hps->ihp/dot_general | solution.py:76
  81.4 1.7 %copy.69 = f32[256,1280]{1,0:T(8,128)S(1)} copy(f32[256,1280]{0,1:T(8,128)} %bitcast.84) | data formatting | bytes 2621440 | tf_op jit(solution)/shard_map/concatenate | solution.py:137
  83.5 0.9 copy-done.2
  84.4 2.2 %fusion.21 = f32[256,20,64]{0,2,1:T(8,128)} fusion(f32[256,20,64]{0,2,1:T(8,128)S(1)} %copy-done.2, f32[256,20,64]{0,2,1:T(8,128)S(1)} %fusion.38, f32[256,20]{0,1:T(8,128)} %get-tuple-element.25, bf16[20,64,128]{2,1,0:T(8,128)(2,1)S(1)} %collective-permute-done.1, bf16[20,64,128]{2,1,0:T(8,128)(2,1)S(1)} %collective-permute-done.2, f32[20]{0:T(128)S(1)} %exp.71, ...), kind=kOutput, calls=%fused_computation.34 | convolution fusion | flops 85688320 | bytes 4674048 | tf_op jit(solution)/shard_map/is,hps->ihp/dot_general | solution.py:75
  86.6 2.8 %copy.68 = f32[256,1280]{1,0:T(8,128)} copy(f32[256,1280]{0,1:T(8,128)} %bitcast.83) | data formatting | bytes 2621440 | tf_op jit(solution)/shard_map/concatenate | solution.py:137
  89.4 4.2 %multiply_reduce_fusion = (f32[512]{0:T(512)S(1)}, f32[512,1280]{1,0:T(8,128)}) fusion(bf16[512,1280]{1,0:T(8,128)(2,1)} %param.14, bf16[512,1280]{1,0:T(8,128)(2,1)S(1)} %divide_convert_fusion, f32[1280]{0:T(1024)S(1)} %mul.340, f32[256,1280]{1,0:T(8,128)S(1)} %copy.69, f32[256,1280]{1,0:T(8,128)} %copy.68), kind=kLoop, calls=%fused_computation.12 | loop fusion | flops 7208448 | bytes 7871488 | tf_op jit(solution)/shard_map/reduce_sum | solution.py:141
  93.7 5.8 %psum.7 = f32[512]{0:T(512)S(1)} all-reduce(f32[512]{0:T(512)S(1)} %get-tuple-element.12), channel_id=1, replica_groups=mesh['groups'=2,'seq'=4,'tensor'=4] {'tensor'}, use_global_device_ids=true, to_apply=%region_5.6 | all-reduce | flops 512 | bytes 4096 | tf_op jit(solution)/shard_map/psum | solution.py:141
  99.5 2.0 %multiply_convert_fusion.4 = bf16[512,1280]{1,0:T(8,128)(2,1)S(1)} fusion(f32[512,1280]{1,0:T(8,128)} %get-tuple-element.13, f32[1280]{0:T(1024)S(1)} %copy-done.14, f32[512]{0:T(512)S(1)} %add_rsqrt_fusion), kind=kLoop, calls=%fused_computation.11 | loop fusion | flops 1966080 | bytes 3939328 | tf_op jit(solution)/shard_map/convert_element_type | solution.py:145
  101.6 0.9 gather_fusion
  104.4 0.7 reshape.263
  105.1 4.7 %all-to-all-start = ((f32[4,1,640]{2,1,0:T(1,128)}), f32[4,1,640]{2,1,0:T(1,128)S(1)}, u32[]{:S(2)}, u32[]{:S(2)}) async-start(f32[4,1,640]{2,1,0:T(1,128)} %reshape.263), calls=%async_computation | async-start | bytes 20480 | tf_op jit(solution)/shard_map/all_to_all | solution.py:173
  110.7 1.4 %convert_element_type.154 = bf16[4,40,1280]{2,1,0:T(8,128)(2,1)} reshape(bf16[160,8,160]{2,1,0:T(8,128)(2,1)S(1)} %copy.75) | data formatting | bytes 819200 | tf_op jit(solution)/shard_map/convert_element_type | solution.py:170
  112.2 3.2 %all-to-all-done = f32[4,1,640]{2,1,0:T(1,128)S(1)} async-done(((f32[4,1,640]{2,1,0:T(1,128)}), f32[4,1,640]{2,1,0:T(1,128)S(1)}, u32[]{:S(2)}, u32[]{:S(2)}) %all-to-all-start) | async-done | bytes 10272 | tf_op jit(solution)/shard_map/all_to_all | solution.py:173
  115.3 3.5 %all-to-all-start.1 = ((bf16[4,40,1280]{2,1,0:T(8,128)(2,1)}), bf16[4,40,1280]{2,1,0:T(8,128)(2,1)S(1)}, u32[]{:S(2)}, u32[]{:S(2)}) async-start(bf16[4,40,1280]{2,1,0:T(8,128)(2,1)} %convert_element_type.154), calls=%async_computation.1 | async-start | bytes 819200 | tf_op jit(solution)/shard_map/all_to_all | solution.py:169
  119.3 0.7 reduce.18
  120.4 0.6 mul.355
  121.4 8.3 %all-to-all-done.1 = bf16[4,40,1280]{2,1,0:T(8,128)(2,1)S(1)} async-done(((bf16[4,40,1280]{2,1,0:T(8,128)(2,1)}), bf16[4,40,1280]{2,1,0:T(8,128)(2,1)S(1)}, u32[]{:S(2)}, u32[]{:S(2)}) %all-to-all-start.1) | async-done | bytes 409632 | tf_op jit(solution)/shard_map/all_to_all | solution.py:169
  129.7 0.7 div.33
  (94 shorter events, 8.1 us)
Async XLA Ops:
  0.6 47.6 %copy-start.1 = (bf16[512,1280]{1,0:T(8,128)(2,1)S(1)}, bf16[512,1280]{1,0:T(8,128)(2,1)}, u32[]{:S(2)}) copy-start(bf16[512,1280]{1,0:T(8,128)(2,1)} %param.13) | copy-start | bytes 3932164
  2.2 46.0 %collective-permute-start = (bf16[3,1536]{1,0:T(4,128)(2,1)S(1)}, bf16[3,1536]{1,0:T(4,128)(2,1)S(1)}, u32[]{:S(2)}, u32[]{:S(2)}) collective-permute-start(bf16[3,1536]{1,0:T(4,128)(2,1)S(1)} %pad_maximum_fusion.3), channel_id=1, source_target_pairs={{0,4},{4,8},{8,12},{1,5},{5,9},{9,13},{2,6},{6,10},{10,14},{3,7},{... | collective-permute-start | bytes 27656 | tf_op jit(solution)/shard_map/ppermute | solution.py:16
  8.9 9.7 %copy-start.6 = (f32[3,8,2,128]{3,1,2,0:T(8,128)}, f32[3,8,2,128]{3,1,2,0:T(8,128)S(1)}, u32[]{:S(2)}) copy-start(f32[3,8,2,128]{3,1,2,0:T(8,128)S(1)} %copy.80) | copy-start | bytes 73732
  9.8 8.8 %copy-start.8 = (f32[3,8,2,128]{3,1,2,0:T(8,128)}, f32[3,8,2,128]{3,1,2,0:T(8,128)S(1)}, u32[]{:S(2)}) copy-start(f32[3,8,2,128]{3,1,2,0:T(8,128)S(1)} %copy.81) | copy-start | bytes 73732
  10.6 37.6 %collective-permute-start.3 = (f32[20]{0:T(128)S(1)}, f32[20]{0:T(128)S(1)}, u32[]{:S(2)}, u32[]{:S(2)}) collective-permute-start(f32[20]{0:T(128)S(1)} %get-tuple-element.33), channel_id=1, source_target_pairs={{0,4},{4,8},{8,12},{1,5},{5,9},{9,13},{2,6},{6,10},{10,14},{3,7},{... | collective-permute-start | bytes 248 | tf_op jit(solution)/shard_map/ppermute | solution.py:16
  53.5 5.5 %copy-start.4 = (f32[256,256]{1,0:T(8,128)S(1)}, f32[256,256]{1,0:T(8,128)}, u32[]{:S(2)}) copy-start(f32[256,256]{1,0:T(8,128)} %fusion.57) | copy-start | bytes 786436
  53.5 5.5 %copy-start.9 = (f32[3,8,2,128]{3,1,2,0:T(8,128)S(1)}, f32[3,8,2,128]{3,1,2,0:T(8,128)}, u32[]{:S(2)}) copy-start(f32[3,8,2,128]{3,1,2,0:T(8,128)} %copy-done.8) | copy-start | bytes 73732
  53.5 5.5 %copy-start.11 = (pred[256,256]{1,0:T(8,128)(4,1)S(1)}, pred[256,256]{1,0:T(8,128)(4,1)}, u32[]{:S(2)}) copy-start(pred[256,256]{1,0:T(8,128)(4,1)} %iota_compare_fusion) | copy-start | bytes 196612
  53.5 5.5 %copy-start.13 = (f32[20,256]{1,0:T(8,128)S(1)}, f32[20,256]{1,0:T(8,128)}, u32[]{:S(2)}) copy-start(f32[20,256]{1,0:T(8,128)} %get-tuple-element.21) | copy-start | bytes 61444
  55.7 9.1 %collective-permute-start.1 = (bf16[20,64,128]{2,1,0:T(8,128)(2,1)S(1)}, bf16[20,64,128]{2,1,0:T(8,128)(2,1)S(1)}, u32[]{:S(2)}, u32[]{:S(2)}) collective-permute-start(bf16[20,64,128]{2,1,0:T(8,128)(2,1)S(1)} %get-tuple-element.35), channel_id=1, source_target_pairs={{0,4},{4,8},{8,12},{1,5},{5,9},{9,13},{2,6},{6,10},{10,14},{3,7},{... | collective-permute-start | bytes 983048 | tf_op jit(solution)/shard_map/ppermute | solution.py:16
  59.0 5.8 %copy-start.16 = (f32[20]{0:T(128)S(1)}, f32[20]{0:T(128)}, u32[]{:S(2)}) copy-start(f32[20]{0:T(128)} %get-tuple-element.32) | copy-start | bytes 244
  59.0 15.9 %copy-start.7 = (f32[3,8,2,128]{3,1,2,0:T(8,128)S(1)}, f32[3,8,2,128]{3,1,2,0:T(8,128)}, u32[]{:S(2)}) copy-start(f32[3,8,2,128]{3,1,2,0:T(8,128)} %copy-done.6) | copy-start | bytes 73732
  59.0 15.9 %copy-start.12 = (f32[20,256]{1,0:T(8,128)S(1)}, f32[20,256]{1,0:T(8,128)}, u32[]{:S(2)}) copy-start(f32[20,256]{1,0:T(8,128)} %get-tuple-element.18) | copy-start | bytes 61444
  65.0 14.5 %collective-permute-start.2 = (bf16[20,64,128]{2,1,0:T(8,128)(2,1)S(1)}, bf16[20,64,128]{2,1,0:T(8,128)(2,1)S(1)}, u32[]{:S(2)}, u32[]{:S(2)}) collective-permute-start(bf16[20,64,128]{2,1,0:T(8,128)(2,1)S(1)} %fusion.29), channel_id=1, source_target_pairs={{0,8},{4,12},{1,9},{5,13},{2,10},{6,14},{3,11},{7,15},{16,24},{20,... | collective-permute-start | bytes 983048 | tf_op jit(solution)/shard_map/ppermute | solution.py:16
  75.0 4.5 %copy-start.15 = (f32[20]{0:T(128)S(1)}, f32[20]{0:T(128)}, u32[]{:S(2)}) copy-start(f32[20]{0:T(128)} %get-tuple-element.30) | copy-start | bytes 244
  77.9 2.0 %copy-start.10 = (f32[256,20]{0,1:T(8,128)S(1)}, f32[256,20]{0,1:T(8,128)}, u32[]{:S(2)}) copy-start(f32[256,20]{0,1:T(8,128)} %get-tuple-element.24) | copy-start | bytes 61444
  83.1 1.3 %copy-start.2 = (f32[256,20,64]{0,2,1:T(8,128)S(1)}, f32[256,20,64]{0,2,1:T(8,128)}, u32[]{:S(2)}) copy-start(f32[256,20,64]{0,2,1:T(8,128)} %fusion.18) | copy-start | bytes 3932164
  89.4 10.1 %copy-start.14 = (f32[1280]{0:T(1024)S(1)}, f32[1280]{0:T(1024)}, u32[]{:S(2)}) copy-start(f32[1280]{0:T(1024)} %param.21) | copy-start | bytes 15364
  101.5 2.1 %copy-start = (bf16[512,1280]{1,0:T(8,128)(2,1)}, bf16[512,1280]{1,0:T(8,128)(2,1)S(1)}, u32[]{:S(2)}) copy-start(bf16[512,1280]{1,0:T(8,128)(2,1)S(1)} %multiply_convert_fusion.4) | copy-start | bytes 3932164
  101.5 1.6 %copy-start.3 = (bf16[160,8,160]{2,1,0:T(8,128)(2,1)S(1)}, bf16[160,8,160]{2,1,0:T(8,128)(2,1)}, u32[]{:S(2)}) copy-start(bf16[160,8,160]{2,1,0:T(8,128)(2,1)} %reshape.222) | copy-start | bytes 1228804
  101.6 1.6 %copy-start.5 = (pred[160,128]{1,0:T(8,128)(4,1)S(1)}, pred[160,128]{1,0:T(8,128)(4,1)}, u32[]{:S(2)}) copy-start(pred[160,128]{1,0:T(8,128)(4,1)} %compare_and_fusion) | copy-start | bytes 61444
  101.6 1.5 %copy-start.17 = (pred[128]{0:T(512)(128)(4,1)S(1)}, pred[128]{0:T(512)(128)(4,1)}, u32[]{:S(2)}) copy-start(pred[128]{0:T(512)(128)(4,1)} %get-tuple-element.10) | copy-start | bytes 388
  105.1 10.2 %all-to-all-start = ((f32[4,1,640]{2,1,0:T(1,128)}), f32[4,1,640]{2,1,0:T(1,128)S(1)}, u32[]{:S(2)}, u32[]{:S(2)}) async-start(f32[4,1,640]{2,1,0:T(1,128)} %reshape.263), calls=%async_computation | async-start | bytes 20480 | tf_op jit(solution)/shard_map/all_to_all | solution.py:173
  115.3 14.3 %all-to-all-start.1 = ((bf16[4,40,1280]{2,1,0:T(8,128)(2,1)}), bf16[4,40,1280]{2,1,0:T(8,128)(2,1)S(1)}, u32[]{:S(2)}, u32[]{:S(2)}) async-start(bf16[4,40,1280]{2,1,0:T(8,128)(2,1)} %convert_element_type.154), calls=%async_computation.1 | async-start | bytes 819200 | tf_op jit(solution)/shard_map/all_to_all | solution.py:169
where the time goes:
time: 132 us; the launch traced here: 130 us
  starting transfers between devices  29.8 us (23%)
  blocking collectives  27.6 us (21%)
  other arithmetic  20.7 us (16%)
  local copies, waits for them, and re-layouts  20.5 us (16%)
  waiting for transfers between devices  16.9 us (13%)
  matrix products  13.3 us (10%)
  between operations  1.74 us (1%)
    ppermute x4, starting transfers between devices, passed_along(): lax.ppermute(value, axis, [(source, source + steps) for source in range(l...  21.6 us
    all_gather x1, blocking collectives, local(): queries_all = lax.all_gather(pool_query, 'seq', axis=0, tiled=True)  15.2 us
    all_to_all x1, waiting for transfers between devices, local(): lax.all_to_all(numer.reshape(pools_all, channels).astype(jnp.bfloat16), '...  8.25 us
    unnamed x1, blocking collectives  6.55 us
    psum x1, blocking collectives, local(): square_sum = lax.psum(jnp.sum(gated * gated, axis=1), 'tensor')  5.81 us
    ppermute x4, waiting for transfers between devices, passed_along(): lax.ppermute(value, axis, [(source, source + steps) for source in range(l...  5.47 us
    unnamed x47, local copies, waits for them, and re-layouts  5.14 us
    all_to_all x1, starting transfers between devices, local(): stats_sent = lax.all_to_all(stats, 'seq', 0, 0, tiled=True)  4.65 us
  transfers between devices with their start and end apart: 6, of which 4 were waited for; matrix products, arithmetic and copies ran while one was open for 19% of the time, Pallas kernels for 0%

commit v1 on v0

--- a/solution.py
+++ b/solution.py
@@ -1,3 +1,4 @@
+import functools
 import math
 import jax
 import jax.numpy as jnp
@@ -8,6 +9,28 @@
 POOL_HEADS = 32
 EPSILON = 1e-05
 MASKED = -1e30
+
+
+def refer_page(vals, mesh_dim):
+    y = jax.lax.axis_size(mesh_dim)
+    f_next, local_now = (y, jax.lax.axis_index(mesh_dim))
+    answer = vals.shape[0] // f_next
+    shaped = list(vals.shape)
+    shaped[0] = answer
+    front = shaped[0]
+    shaped[0] = front * f_next
+    tmp = jnp.zeros(shaped, vals.dtype)
+    for i in range(f_next):
+        heard = lax.dynamic_slice_in_dim(vals, (local_now ^ i) * answer, answer, axis=0)
+        if i:
+            heard = jax.lax.ppermute(
+                heard, mesh_dim, list(map(lambda hop_no: (hop_no, hop_no ^ i), range(f_next)))
+            )
+        tmp = lax.dynamic_update_slice_in_dim(tmp, heard, (local_now ^ i) * front, axis=0)
+    return tmp
+
+
+lead_rings = functools.partial(refer_page, mesh_dim="seq")
 
 
 def passed_along(value, axis, steps):
@@ -166,9 +189,7 @@
     numer = jnp.einsum(
         "apr,rad->pad", expo.astype(jnp.bfloat16), keys_block, preferred_element_type=jnp.float32
     )
-    numer_sent = lax.all_to_all(
-        numer.reshape(pools_all, channels).astype(jnp.bfloat16), "seq", 0, 0, tiled=True
-    )
+    numer_sent = lead_rings(numer.reshape(pools_all, channels).astype(jnp.bfloat16))
     stats = jnp.concatenate([peak.T, denom.T], axis=1)
     stats_sent = lax.all_to_all(stats, "seq", 0, 0, tiled=True)
     numer_parts = numer_sent.astype(jnp.float32).reshape(

time: 132 us -> 125 us (0.947)
  waiting for transfers between devices: 16.9 us -> 11 us
    all_to_all x1 -> x0, waiting for transfers between devices: 8.25 us -> none  [local(): lax.all_to_all(numer.reshape(pools_all, channels).astype(jnp.bfloat16), '...]
    ppermute x0 -> x3, starting transfers between devices: none -> 5.01 us  [refer_page(): jax.lax.ppermute(heard, mesh_dim, list(map(lambda hop_no: (hop_no, hop_no...]
    all_to_all x1 -> x0, starting transfers between devices: 3.46 us -> none  [local(): lax.all_to_all(numer.reshape(pools_all, channels).astype(jnp.bfloat16), '...]
    all_to_all x1, waiting for transfers between devices: 3.16 us -> 5.54 us  [local(): stats_sent = lax.all_to_all(stats, 'seq', 0, 0, tiled=True)]
    convert_element_type x2 -> x0, local copies, waits for them, and re-layouts: 1.99 us -> none  [local(): numer.reshape(pools_all, channels).astype(jnp.bfloat16)]
    unnamed x47 -> x51, local copies, waits for them, and re-layouts: 5.14 us -> 5.77 us
  transfers between devices with their start and end apart: 6 -> 8, of which waited for: 4 -> 3; matrix products, arithmetic and copies ran while one was open for 19% -> 18% of each run, Pallas kernels for 0% -> 0%
where the time goes in v1:
time: 125 us; the launch traced here: 124 us
  starting transfers between devices  30.3 us (24%)
  blocking collectives  27.6 us (22%)
  local copies, waits for them, and re-layouts  20.3 us (16%)
  other arithmetic  20.2 us (16%)
  matrix products  13.4 us (11%)
  waiting for transfers between devices  11 us (9%)
  between operations  1.77 us (1%)
    ppermute x4, starting transfers between devices, passed_along(): lax.ppermute(value, axis, [(source, source + steps) for source in range(l...  21.6 us
    all_gather x1, blocking collectives, local(): queries_all = lax.all_gather(pool_query, 'seq', axis=0, tiled=True)  15.2 us
    unnamed x1, blocking collectives  6.55 us
    psum x1, blocking collectives, local(): square_sum = lax.psum(jnp.sum(gated * gated, axis=1), 'tensor')  5.81 us
    unnamed x51, local copies, waits for them, and re-layouts  5.77 us
    all_to_all x1, waiting for transfers between devices, local(): stats_sent = lax.all_to_all(stats, 'seq', 0, 0, tiled=True)  5.54 us
    ppermute x4, waiting for transfers between devices, passed_along(): lax.ppermute(value, axis, [(source, source + steps) for source in range(l...  5.47 us
    ppermute x3, starting transfers between devices, refer_page(): jax.lax.ppermute(heard, mesh_dim, list(map(lambda hop_no: (hop_no, hop_no...  5.01 us
  transfers between devices with their start and end apart: 8, of which 3 were waited for; matrix products, arithmetic and copies ran while one was open for 18% of the time, Pallas kernels for 0%

profile of v1, /device:TPU:0, one launch (start us, length us, event | category | flops | bytes accessed | tf_op | source)
XLA Modules:
  0.0 124.5 jit_solution(18262248038066140282)
XLA Ops:
  0.6 0.8 slice.127
  1.4 0.7 slice.126
  2.2 5.0 %collective-permute-start = (bf16[3,1536]{1,0:T(4,128)(2,1)S(1)}, bf16[3,1536]{1,0:T(4,128)(2,1)S(1)}, u32[]{:S(2)}, u32[]{:S(2)}) collective-permute-start(bf16[3,1536]{1,0:T(4,128)(2,1)S(1)} %pad_maximum_fusion.3), channel_id=1, source_target_pairs={{0,4},{4,8},{8,12},{1,5},{5,9},{9,13},{2,6},{6,10},{10,14},{3,7},{... | collective-permute-start | bytes 27656 | tf_op jit(solution)/shard_map/ppermute | solution.py:39
  7.2 0.8 fusion.81
  7.9 0.6 reduce-window.14
  8.9 0.6 reduce-window.16
  10.6 3.5 %collective-permute-start.3 = (f32[20]{0:T(128)S(1)}, f32[20]{0:T(128)S(1)}, u32[]{:S(2)}, u32[]{:S(2)}) collective-permute-start(f32[20]{0:T(128)S(1)} %get-tuple-element.37), channel_id=1, source_target_pairs={{0,4},{4,8},{8,12},{1,5},{5,9},{9,13},{2,6},{6,10},{10,14},{3,7},{... | collective-permute-start | bytes 248 | tf_op jit(solution)/shard_map/ppermute | solution.py:39
  14.1 0.7 iota_compare_fusion
  14.8 0.9 convert_reduce_fusion.3
  15.7 1.5 %fusion.80 = (f32[20,256]{1,0:T(8,128)}, f32[256,20]{0,1:T(8,128)}, f32[256,20]{0,1:T(8,128)}, f32[20,256]{1,0:T(8,128)}, f32[256,20]{0,1:T(8,128)}, /*index=5*/f32[256,20]{0,1:T(8,128)}) fusion(f32[20,512]{1,0:T(8,128)} %param.16, f32[20,256]{1,0:T(8,128)S(1)} %bitcast.90, f32[20]{0:T(128)S(1)} %get-tuple-element.43, f32[20,256]{1,0:T(8,128)S(1)} %bitcast.93, ...), kind=kLoop, calls=%fused_computation.148 | loop fusion | flops 20480 | bytes 204960 | tf_op jit(solution)/shard_map/slice | solution.py:146
  17.2 1.4 %slice_convert_fusion.3 = (f32[1,256]{1,0:T(1,128)}, f32[1,256]{1,0:T(1,128)}, f32[1,256]{1,0:T(1,128)}, f32[1,256]{1,0:T(1,128)}) fusion(bf16[4,256]{1,0:T(4,128)(2,1)} %param.20), kind=kLoop, calls=%fused_computation.138 | loop fusion | flops 1024 | bytes 6144 | tf_op jit(solution)/shard_map/mul | solution.py:52
  18.6 15.2 %all_gather.11 = bf16[160,1280]{1,0:T(8,128)(2,1)S(1)} all-gather(bf16[40,1280]{1,0:T(8,128)(2,1)} %param.23), channel_id=1, replica_groups=mesh['groups'=2,'seq'=4,'tensor'=4] {'seq'}, dimensions={0}, use_global_device_ids=true | all-gather | bytes 512000 | tf_op jit(solution)/shard_map/all_gather | solution.py:125
  33.8 1.2 compare_and_fusion.1
  35.0 1.2 dynamic-slice
  36.8 0.9 dynamic-update-slice.1
  37.6 0.8 dynamic-update-slice
  38.5 6.6 %all-reduce.2 = (s32[160]{0:T(256)S(1)}, s32[160]{0:T(256)S(1)}) all-reduce(s32[160]{0:T(256)S(1)} %dynamic-update-slice.1, s32[160]{0:T(256)S(1)} %dynamic-update-slice), channel_id=1, replica_groups=mesh['groups'=2,'seq'=4,'tensor'=4] {'seq'}, use_global_device_ids=true, to_apply=%add.1 | all-reduce | flops 320 | bytes 2560
  45.0 0.7 compare_and_fusion
  45.7 0.7 mul.352
  46.5 1.7 %reshape.221 = bf16[160,8,160]{2,1,0:T(8,128)(2,1)} reshape(bf16[160,1280]{1,0:T(8,128)(2,1)S(1)} %all_gather.11) | data formatting | bytes 819200 | tf_op jit(solution)/shard_map/reshape | solution.py:177
  48.2 1.8 %divide_convert_fusion = bf16[512,1280]{1,0:T(8,128)(2,1)S(1)} fusion(bf16[512,1280]{1,0:T(8,128)(2,1)S(1)} %copy-done.1, bf16[3,1280]{1,0:T(4,128)(2,1)S(1)} %slice.166, f32[1280]{0:T(1024)S(1)} %get-tuple-element.4, f32[1280]{0:T(1024)S(1)} %get-tuple-element.5, f32[1280]{0:T(1024)S(1)} %get-tuple-element.3, f32[1280]{0:T(1024)S(1)} %get-tuple-element.2), kind=kLoop, calls=%fused_computation.23 | loop fusion | flops 15728640 | bytes 2649600 | tf_op jit(solution)/shard_map/convert_element_type | solution.py:55
  50.4 1.9 %divide_convert_fusion.1 = bf16[512,256]{1,0:T(8,128)(2,1)S(1)} fusion(bf16[512,256]{1,0:T(8,128)(2,1)} %param.15, bf16[3,256]{1,0:T(4,128)(2,1)S(1)} %slice.173, f32[256]{0:T(256)} %bitcast.102, f32[256]{0:T(256)} %bitcast.103, f32[256]{0:T(256)} %bitcast.101, f32[256]{0:T(256)} %bitcast.100), kind=kLoop, calls=%fused_computation.61 | loop fusion | flops 3145728 | bytes 529920 | tf_op jit(solution)/shard_map/convert_element_type | solution.py:55
  52.3 0.9 fusion.56
  53.5 1.1 convolution_add_fusion.3
  54.6 1.1 fusion.83
  55.7 3.3 %collective-permute-start.1 = (bf16[20,64,128]{2,1,0:T(8,128)(2,1)S(1)}, bf16[20,64,128]{2,1,0:T(8,128)(2,1)S(1)}, u32[]{:S(2)}, u32[]{:S(2)}) collective-permute-start(bf16[20,64,128]{2,1,0:T(8,128)(2,1)S(1)} %get-tuple-element.39), channel_id=1, source_target_pairs={{0,4},{4,8},{8,12},{1,5},{5,9},{9,13},{2,6},{6,10},{10,14},{3,7},{... | collective-permute-start | bytes 983048 | tf_op jit(solution)/shard_map/ppermute | solution.py:39
  59.1 1.7 %fusion.17 = f32[256,20,64]{0,2,1:T(8,128)S(1)} fusion(bf16[256,20,64]{0,2,1:T(8,128)(2,1)S(1)} %bitcast.86, f32[20,256]{1,0:T(8,128)S(1)} %copy-done.13, f32[256,256]{1,0:T(8,128)S(1)} %copy-done.4, f32[20,256]{1,0:T(8,128)S(1)} %bitcast.94, pred[256,256]{1,0:T(8,128)(4,1)S(1)} %copy-done.11), kind=kOutput, calls=%fused_computation.28 | convolution fusion | flops 175636480 | bytes 2334720 | tf_op jit(solution)/shard_map/hij,jhp->ihp/dot_general | solution.py:68
  60.9 3.9 %collective-permute-done.1 = bf16[20,64,128]{2,1,0:T(8,128)(2,1)S(1)} collective-permute-done((bf16[20,64,128]{2,1,0:T(8,128)(2,1)S(1)}, bf16[20,64,128]{2,1,0:T(8,128)(2,1)S(1)}, u32[]{:S(2)}, u32[]{:S(2)}) %collective-permute-start.1) | collective-permute-done | bytes 327712 | tf_op jit(solution)/shard_map/ppermute | solution.py:39
  65.0 10.0 %collective-permute-start.2 = (bf16[20,64,128]{2,1,0:T(8,128)(2,1)S(1)}, bf16[20,64,128]{2,1,0:T(8,128)(2,1)S(1)}, u32[]{:S(2)}, u32[]{:S(2)}) collective-permute-start(bf16[20,64,128]{2,1,0:T(8,128)(2,1)S(1)} %fusion.28), channel_id=1, source_target_pairs={{0,8},{4,12},{1,9},{5,13},{2,10},{6,14},{3,11},{7,15},{16,24},{20,... | collective-permute-start | bytes 983048 | tf_op jit(solution)/shard_map/ppermute | solution.py:39
  75.0 2.9 %fusion.18 = f32[256,20,64]{0,2,1:T(8,128)} fusion(bf16[256,20,64]{0,2,1:T(8,128)(2,1)S(1)} %bitcast.84, f32[20,256]{1,0:T(8,128)S(1)} %copy-done.12, f32[256,256]{1,0:T(8,128)S(1)} %fusion.60, f32[20,256]{1,0:T(8,128)S(1)} %bitcast.91, pred[256,256]{1,0:T(8,128)(4,1)S(1)} %copy-done.11), kind=kOutput, calls=%fused_computation.29 | convolution fusion | flops 175636480 | bytes 2334720 | tf_op jit(solution)/shard_map/hij,jhp->ihp/dot_general | solution.py:68
  77.9 1.6 %collective-permute-done.2 = bf16[20,64,128]{2,1,0:T(8,128)(2,1)S(1)} collective-permute-done((bf16[20,64,128]{2,1,0:T(8,128)(2,1)S(1)}, bf16[20,64,128]{2,1,0:T(8,128)(2,1)S(1)}, u32[]{:S(2)}, u32[]{:S(2)}) %collective-permute-start.2) | collective-permute-done | bytes 327712 | tf_op jit(solution)/shard_map/ppermute | solution.py:39
  79.9 1.5 %fusion.22 = f32[256,20,64]{0,2,1:T(8,128)} fusion(f32[256,20,64]{0,2,1:T(8,128)S(1)} %fusion.17, f32[256,20,64]{0,2,1:T(8,128)S(1)} %fusion.48, f32[256,20]{0,1:T(8,128)S(1)} %copy-done.10, bf16[512,256]{1,0:T(8,128)(2,1)S(1)} %divide_convert_fusion.1, f32[20,64,128]{2,1,0:T(8,128)S(1)} %convolution_add_fusion.3, ...), kind=kOutput, calls=%fused_computation.35 | convolution fusion | flops 86507520 | bytes 5334016 | tf_op jit(solution)/shard_map/is,hps->ihp/dot_general | solution.py:99
  81.4 1.7 %copy.76 = f32[256,1280]{1,0:T(8,128)S(1)} copy(f32[256,1280]{0,1:T(8,128)} %bitcast.82) | data formatting | bytes 2621440 | tf_op jit(solution)/shard_map/concatenate | solution.py:160
  83.5 0.9 copy-done.2
  84.4 2.2 %fusion.21 = f32[256,20,64]{0,2,1:T(8,128)} fusion(f32[256,20,64]{0,2,1:T(8,128)S(1)} %copy-done.2, f32[256,20,64]{0,2,1:T(8,128)S(1)} %fusion.37, f32[256,20]{0,1:T(8,128)} %get-tuple-element.29, bf16[20,64,128]{2,1,0:T(8,128)(2,1)S(1)} %collective-permute-done.1, bf16[20,64,128]{2,1,0:T(8,128)(2,1)S(1)} %collective-permute-done.2, f32[20]{0:T(128)S(1)} %exp.71, ...), kind=kOutput, calls=%fused_computation.34 | convolution fusion | flops 85688320 | bytes 4674048 | tf_op jit(solution)/shard_map/is,hps->ihp/dot_general | solution.py:98
  86.6 2.8 %copy.75 = f32[256,1280]{1,0:T(8,128)} copy(f32[256,1280]{0,1:T(8,128)} %bitcast.81) | data formatting | bytes 2621440 | tf_op jit(solution)/shard_map/concatenate | solution.py:160
  89.4 4.2 %multiply_reduce_fusion = (f32[512]{0:T(512)S(1)}, f32[512,1280]{1,0:T(8,128)}) fusion(bf16[512,1280]{1,0:T(8,128)(2,1)} %param.14, bf16[512,1280]{1,0:T(8,128)(2,1)S(1)} %divide_convert_fusion, f32[1280]{0:T(1024)S(1)} %mul.353, f32[256,1280]{1,0:T(8,128)S(1)} %copy.76, f32[256,1280]{1,0:T(8,128)} %copy.75), kind=kLoop, calls=%fused_computation.12 | loop fusion | flops 7208448 | bytes 7871488 | tf_op jit(solution)/shard_map/reduce_sum | solution.py:164
  93.7 5.8 %psum.7 = f32[512]{0:T(512)S(1)} all-reduce(f32[512]{0:T(512)S(1)} %get-tuple-element.12), channel_id=1, replica_groups=mesh['groups'=2,'seq'=4,'tensor'=4] {'tensor'}, use_global_device_ids=true, to_apply=%region_5.6 | all-reduce | flops 512 | bytes 4096 | tf_op jit(solution)/shard_map/psum | solution.py:164
  99.5 2.0 %multiply_convert_fusion.4 = bf16[512,1280]{1,0:T(8,128)(2,1)S(1)} fusion(f32[512,1280]{1,0:T(8,128)} %get-tuple-element.13, f32[1280]{0:T(1024)S(1)} %copy-done.14, f32[512]{0:T(512)S(1)} %add_rsqrt_fusion), kind=kLoop, calls=%fused_computation.11 | loop fusion | flops 1966080 | bytes 3939328 | tf_op jit(solution)/shard_map/convert_element_type | solution.py:168
  101.6 0.9 gather_fusion
  105.8 3.4 %collective-permute-start.5 = (bf16[40,1280]{1,0:T(8,128)(2,1)S(1)}, bf16[40,1280]{1,0:T(8,128)(2,1)S(1)}, u32[]{:S(2)}, u32[]{:S(2)}) collective-permute-start(bf16[40,1280]{1,0:T(8,128)(2,1)S(1)} %copy.90), channel_id=1, source_target_pairs={{0,8},{4,12},{8,0},{12,4},{1,9},{5,13},{9,1},{13,5},{2,10},{6,14},... | collective-permute-start | bytes 307208 | tf_op jit(solution)/shard_map/ppermute | solution.py:26
  109.4 1.5 %collective-permute-start.6 = (bf16[40,1280]{1,0:T(8,128)(2,1)S(1)}, bf16[40,1280]{1,0:T(8,128)(2,1)S(1)}, u32[]{:S(2)}, u32[]{:S(2)}) collective-permute-start(bf16[40,1280]{1,0:T(8,128)(2,1)S(1)} %copy.91), channel_id=1, source_target_pairs={{0,12},{4,8},{8,4},{12,0},{1,13},{5,9},{9,5},{13,1},{2,14},{6,10},... | collective-permute-start | bytes 307208 | tf_op jit(solution)/shard_map/ppermute | solution.py:26
  111.0 0.7 reshape.266
  111.7 3.6 %all-to-all-start = ((f32[4,1,640]{2,1,0:T(1,128)}), f32[4,1,640]{2,1,0:T(1,128)S(1)}, u32[]{:S(2)}, u32[]{:S(2)}) async-start(f32[4,1,640]{2,1,0:T(1,128)} %reshape.266), calls=%async_computation | async-start | bytes 20480 | tf_op jit(solution)/shard_map/all_to_all | solution.py:194
  115.4 5.5 %all-to-all-done = f32[4,1,640]{2,1,0:T(1,128)S(1)} async-done(((f32[4,1,640]{2,1,0:T(1,128)}), f32[4,1,640]{2,1,0:T(1,128)S(1)}, u32[]{:S(2)}, u32[]{:S(2)}) %all-to-all-start) | async-done | bytes 10272 | tf_op jit(solution)/shard_map/all_to_all | solution.py:194
  121.4 0.7 reduce.17
  122.5 0.8 reshape.234
  123.6 0.8 div.34
  (104 shorter events, 8.0 us)
Async XLA Ops:
  0.6 47.6 %copy-start.1 = (bf16[512,1280]{1,0:T(8,128)(2,1)S(1)}, bf16[512,1280]{1,0:T(8,128)(2,1)}, u32[]{:S(2)}) copy-start(bf16[512,1280]{1,0:T(8,128)(2,1)} %param.13) | copy-start | bytes 3932164
  2.2 46.0 %collective-permute-start = (bf16[3,1536]{1,0:T(4,128)(2,1)S(1)}, bf16[3,1536]{1,0:T(4,128)(2,1)S(1)}, u32[]{:S(2)}, u32[]{:S(2)}) collective-permute-start(bf16[3,1536]{1,0:T(4,128)(2,1)S(1)} %pad_maximum_fusion.3), channel_id=1, source_target_pairs={{0,4},{4,8},{8,12},{1,5},{5,9},{9,13},{2,6},{6,10},{10,14},{3,7},{... | collective-permute-start | bytes 27656 | tf_op jit(solution)/shard_map/ppermute | solution.py:39
  8.9 9.7 %copy-start.6 = (f32[3,8,2,128]{3,1,2,0:T(8,128)}, f32[3,8,2,128]{3,1,2,0:T(8,128)S(1)}, u32[]{:S(2)}) copy-start(f32[3,8,2,128]{3,1,2,0:T(8,128)S(1)} %copy.92) | copy-start | bytes 73732
  9.8 8.8 %copy-start.8 = (f32[3,8,2,128]{3,1,2,0:T(8,128)}, f32[3,8,2,128]{3,1,2,0:T(8,128)S(1)}, u32[]{:S(2)}) copy-start(f32[3,8,2,128]{3,1,2,0:T(8,128)S(1)} %copy.93) | copy-start | bytes 73732
  10.6 37.6 %collective-permute-start.3 = (f32[20]{0:T(128)S(1)}, f32[20]{0:T(128)S(1)}, u32[]{:S(2)}, u32[]{:S(2)}) collective-permute-start(f32[20]{0:T(128)S(1)} %get-tuple-element.37), channel_id=1, source_target_pairs={{0,4},{4,8},{8,12},{1,5},{5,9},{9,13},{2,6},{6,10},{10,14},{3,7},{... | collective-permute-start | bytes 248 | tf_op jit(solution)/shard_map/ppermute | solution.py:39
  53.5 5.5 %copy-start.4 = (f32[256,256]{1,0:T(8,128)S(1)}, f32[256,256]{1,0:T(8,128)}, u32[]{:S(2)}) copy-start(f32[256,256]{1,0:T(8,128)} %fusion.56) | copy-start | bytes 786436
  53.5 5.5 %copy-start.9 = (f32[3,8,2,128]{3,1,2,0:T(8,128)S(1)}, f32[3,8,2,128]{3,1,2,0:T(8,128)}, u32[]{:S(2)}) copy-start(f32[3,8,2,128]{3,1,2,0:T(8,128)} %copy-done.8) | copy-start | bytes 73732
  53.5 5.5 %copy-start.11 = (pred[256,256]{1,0:T(8,128)(4,1)S(1)}, pred[256,256]{1,0:T(8,128)(4,1)}, u32[]{:S(2)}) copy-start(pred[256,256]{1,0:T(8,128)(4,1)} %iota_compare_fusion) | copy-start | bytes 196612
  53.5 5.5 %copy-start.13 = (f32[20,256]{1,0:T(8,128)S(1)}, f32[20,256]{1,0:T(8,128)}, u32[]{:S(2)}) copy-start(f32[20,256]{1,0:T(8,128)} %get-tuple-element.25) | copy-start | bytes 61444
  55.7 9.1 %collective-permute-start.1 = (bf16[20,64,128]{2,1,0:T(8,128)(2,1)S(1)}, bf16[20,64,128]{2,1,0:T(8,128)(2,1)S(1)}, u32[]{:S(2)}, u32[]{:S(2)}) collective-permute-start(bf16[20,64,128]{2,1,0:T(8,128)(2,1)S(1)} %get-tuple-element.39), channel_id=1, source_target_pairs={{0,4},{4,8},{8,12},{1,5},{5,9},{9,13},{2,6},{6,10},{10,14},{3,7},{... | collective-permute-start | bytes 983048 | tf_op jit(solution)/shard_map/ppermute | solution.py:39
  59.0 5.8 %copy-start.16 = (f32[20]{0:T(128)S(1)}, f32[20]{0:T(128)}, u32[]{:S(2)}) copy-start(f32[20]{0:T(128)} %get-tuple-element.36) | copy-start | bytes 244
  59.0 15.9 %copy-start.7 = (f32[3,8,2,128]{3,1,2,0:T(8,128)S(1)}, f32[3,8,2,128]{3,1,2,0:T(8,128)}, u32[]{:S(2)}) copy-start(f32[3,8,2,128]{3,1,2,0:T(8,128)} %copy-done.6) | copy-start | bytes 73732
  59.0 15.9 %copy-start.12 = (f32[20,256]{1,0:T(8,128)S(1)}, f32[20,256]{1,0:T(8,128)}, u32[]{:S(2)}) copy-start(f32[20,256]{1,0:T(8,128)} %get-tuple-element.22) | copy-start | bytes 61444
  65.0 14.5 %collective-permute-start.2 = (bf16[20,64,128]{2,1,0:T(8,128)(2,1)S(1)}, bf16[20,64,128]{2,1,0:T(8,128)(2,1)S(1)}, u32[]{:S(2)}, u32[]{:S(2)}) collective-permute-start(bf16[20,64,128]{2,1,0:T(8,128)(2,1)S(1)} %fusion.28), channel_id=1, source_target_pairs={{0,8},{4,12},{1,9},{5,13},{2,10},{6,14},{3,11},{7,15},{16,24},{20,... | collective-permute-start | bytes 983048 | tf_op jit(solution)/shard_map/ppermute | solution.py:39
  75.0 4.5 %copy-start.15 = (f32[20]{0:T(128)S(1)}, f32[20]{0:T(128)}, u32[]{:S(2)}) copy-start(f32[20]{0:T(128)} %get-tuple-element.34) | copy-start | bytes 244
  77.9 2.0 %copy-start.10 = (f32[256,20]{0,1:T(8,128)S(1)}, f32[256,20]{0,1:T(8,128)}, u32[]{:S(2)}) copy-start(f32[256,20]{0,1:T(8,128)} %get-tuple-element.28) | copy-start | bytes 61444
  83.1 1.3 %copy-start.2 = (f32[256,20,64]{0,2,1:T(8,128)S(1)}, f32[256,20,64]{0,2,1:T(8,128)}, u32[]{:S(2)}) copy-start(f32[256,20,64]{0,2,1:T(8,128)} %fusion.18) | copy-start | bytes 3932164
  89.4 10.1 %copy-start.14 = (f32[1280]{0:T(1024)S(1)}, f32[1280]{0:T(1024)}, u32[]{:S(2)}) copy-start(f32[1280]{0:T(1024)} %param.21) | copy-start | bytes 15364
  101.5 2.1 %copy-start = (bf16[512,1280]{1,0:T(8,128)(2,1)}, bf16[512,1280]{1,0:T(8,128)(2,1)S(1)}, u32[]{:S(2)}) copy-start(bf16[512,1280]{1,0:T(8,128)(2,1)S(1)} %multiply_convert_fusion.4) | copy-start | bytes 3932164
  101.5 1.6 %copy-start.3 = (bf16[160,8,160]{2,1,0:T(8,128)(2,1)S(1)}, bf16[160,8,160]{2,1,0:T(8,128)(2,1)}, u32[]{:S(2)}) copy-start(bf16[160,8,160]{2,1,0:T(8,128)(2,1)} %reshape.221) | copy-start | bytes 1228804
  101.6 1.6 %copy-start.5 = (pred[160,128]{1,0:T(8,128)(4,1)S(1)}, pred[160,128]{1,0:T(8,128)(4,1)}, u32[]{:S(2)}) copy-start(pred[160,128]{1,0:T(8,128)(4,1)} %compare_and_fusion) | copy-start | bytes 61444
  101.6 1.5 %copy-start.17 = (pred[128]{0:T(512)(128)(4,1)S(1)}, pred[128]{0:T(512)(128)(4,1)}, u32[]{:S(2)}) copy-start(pred[128]{0:T(512)(128)(4,1)} %get-tuple-element.10) | copy-start | bytes 388
  105.5 16.9 %collective-permute-start.4 = (bf16[40,1280]{1,0:T(8,128)(2,1)S(1)}, bf16[40,1280]{1,0:T(8,128)(2,1)S(1)}, u32[]{:S(2)}, u32[]{:S(2)}) collective-permute-start(bf16[40,1280]{1,0:T(8,128)(2,1)S(1)} %copy.89), channel_id=1, source_target_pairs={{0,4},{4,0},{8,12},{12,8},{1,5},{5,1},{9,13},{13,9},{2,6},{6,2},{1... | collective-permute-start | bytes 307208 | tf_op jit(solution)/shard_map/ppermute | solution.py:26
  105.8 16.7 %collective-permute-start.5 = (bf16[40,1280]{1,0:T(8,128)(2,1)S(1)}, bf16[40,1280]{1,0:T(8,128)(2,1)S(1)}, u32[]{:S(2)}, u32[]{:S(2)}) collective-permute-start(bf16[40,1280]{1,0:T(8,128)(2,1)S(1)} %copy.90), channel_id=1, source_target_pairs={{0,8},{4,12},{8,0},{12,4},{1,9},{5,13},{9,1},{13,5},{2,10},{6,14},... | collective-permute-start | bytes 307208 | tf_op jit(solution)/shard_map/ppermute | solution.py:26
  109.4 13.1 %collective-permute-start.6 = (bf16[40,1280]{1,0:T(8,128)(2,1)S(1)}, bf16[40,1280]{1,0:T(8,128)(2,1)S(1)}, u32[]{:S(2)}, u32[]{:S(2)}) collective-permute-start(bf16[40,1280]{1,0:T(8,128)(2,1)S(1)} %copy.91), channel_id=1, source_target_pairs={{0,12},{4,8},{8,4},{12,0},{1,13},{5,9},{9,5},{13,1},{2,14},{6,10},... | collective-permute-start | bytes 307208 | tf_op jit(solution)/shard_map/ppermute | solution.py:26
  111.7 9.2 %all-to-all-start = ((f32[4,1,640]{2,1,0:T(1,128)}), f32[4,1,640]{2,1,0:T(1,128)S(1)}, u32[]{:S(2)}, u32[]{:S(2)}) async-start(f32[4,1,640]{2,1,0:T(1,128)} %reshape.266), calls=%async_computation | async-start | bytes 20480 | tf_op jit(solution)/shard_map/all_to_all | solution.py:194
